TPU v7x, 32 devices: a whole 2x2x4 slice. The times are simulated.
32 devices in a mesh: row: 8 (over y, x, core), col: 4 (over z).
Axes of the slice: x: 2, y: 2, z: 4, core: 2. Of those that a mesh axis runs over, the one named last changes fastest.
Arguments:
- magnetic_potential_input: bfloat16 [32, 32768], P('row', 'col'), may hold values from -6 to 6
- node_reordering: int32 [32768], P('col'), may hold values from 0 to 32767, as said below
- adjacent_dense_blocks: bfloat16 [512, 256, 256], P(('row', 'col')), may hold values from -0.375 to 0.375
- adjacent_cluster_pairs: int32 [512, 2], P(('row', 'col')), may hold values from 0 to 127, as said below
- distant_row_factors: bfloat16 [960, 256, 32], P(('row', 'col')), may hold values from -1 to 1
- distant_row_factor_index: int32 [960, 2], P(('row', 'col')), may hold values from 0 to 127, as said below
- distant_column_factors: bfloat16 [960, 256, 32], P(('row', 'col')), may hold values from -0.125 to 0.125
- distant_column_factor_index: int32 [960, 2], P(('row', 'col')), may hold values from 0 to 127, as said below
Outputs:
- field: float32 [32, 32768], P('col', 'row')
Inputs may be any that keep to these rules, and one draw needn't show every extreme that they name: `node_reordering`: each column block of positions k * 32 * 256 to (k + 1) * 32 * 256 - 1 is mapped one to one onto the initial nodes of the same range. `adjacent_cluster_pairs`: slot of device d with row index i: the row cluster lies in i * 16 to (i + 1) * 16 - 1; the column cluster lies within 3 of the row cluster and in column block h = i * (col devices) // (row devices), clusters h * 32 to (h + 1) * 32 - 1. `distant_row_factor_index`: piece of device d with row index i: column 0 is a leaf cluster in i * 16 to (i + 1) * 16 - 1; column 1 is a block slot 0 to 7. A block of level l has 2**l row pieces on 2**l aligned consecutive clusters; each level 0 to 3 has 2 blocks a device. `distant_column_factor_index`: piece of device d with col index j: column 0 is a leaf cluster in j * 32 to (j + 1) * 32 - 1; column 1 is a block slot as in distant_row_factor_index; a block has as many column pieces as row pieces, on aligned consecutive clusters.
All inputs are finite; a program needn't handle non-finite values.
Results may differ from a plain program's by a relative error of at most 0.0023.
Values may be sent and summed in bfloat16 or wider, within the bound.
No kernel may reach another device: no remote copies, remote signals or barrier semaphores. Data moves between devices by JAX's collectives and lax.ppermute only.
A program may use at most 64 MiB of HBM per device.

v0:
```python
import jax
import jax.numpy as jnp
from jax import lax
from jax.sharding import PartitionSpec as P

BL = 2
REACH = 3


def per_device(
    magnetic_potential_input,
    node_reordering,
    adjacent_dense_blocks,
    adjacent_cluster_pairs,
    distant_row_factors,
    distant_row_factor_index,
    distant_column_factors,
    distant_column_factor_index,
):
    row_count = lax.axis_size("row")
    col_count = lax.axis_size("col")
    row_index = lax.axis_index("row")
    col_index = lax.axis_index("col")
    local_states, width = magnetic_potential_input.shape
    states = local_states * row_count
    leaf = adjacent_dense_blocks.shape[1]
    rank = distant_row_factors.shape[2]
    cluster_extent = width // leaf
    row_span = cluster_extent * col_count // row_count
    window = 0
    for target in range(row_count):
        base_t = target * row_span - target * col_count // row_count * cluster_extent
        low_t = max(base_t - REACH, 0)
        high_t = min(base_t + row_span + REACH, cluster_extent)
        window = max(window, high_t - low_t)
    block_entries = 4 * BL
    local_order = node_reordering - col_index * width
    mine = jnp.take(magnetic_potential_input, local_order, axis=1)
    ordered = lax.all_gather(mine, "row", axis=0, tiled=True)
    leaf_clusters = ordered.reshape(states, cluster_extent, leaf)
    every_block = lax.all_gather(mine, "col", axis=0, tiled=False)
    pieces = []
    for target in range(row_count):
        home_t = target * col_count // row_count
        start_t = min(
            max(target * row_span - home_t * cluster_extent - REACH, 0), cluster_extent - window
        )
        pieces.append(every_block[home_t, :, start_t * leaf : (start_t + window) * leaf])
    send = jnp.concatenate(pieces, axis=0)
    near_window = lax.all_to_all(send, "row", 0, 0, tiled=True).reshape(states, window, leaf)
    home = row_index * col_count // row_count
    start = jnp.clip(
        row_index * row_span - home * cluster_extent - REACH, 0, cluster_extent - window
    )
    near_cols = adjacent_cluster_pairs[:, 1] - home * cluster_extent - start
    near_rows = adjacent_cluster_pairs[:, 0] - row_index * row_span
    near_src = jnp.take(near_window, near_cols, axis=1)
    near_out = jnp.einsum(
        "snk,nlk->nsl", near_src, adjacent_dense_blocks, preferred_element_type=jnp.float32
    )
    v_src = jnp.take(
        leaf_clusters, distant_column_factor_index[:, 0] - col_index * cluster_extent, axis=1
    )
    coeffs = jnp.einsum(
        "spk,pkr->psr", v_src, distant_column_factors, preferred_element_type=jnp.float32
    )
    fragments = coeffs.shape[0]
    column_indicator = (
        distant_column_factor_index[:, 1][None, :]
        == jnp.arange(block_entries, dtype=jnp.int32)[:, None]
    ).astype(jnp.float32)
    summed = (
        jnp.dot(
            column_indicator,
            coeffs.reshape(fragments, states * rank),
            precision=lax.Precision.HIGHEST,
        )
        .astype(jnp.bfloat16)
        .reshape(block_entries, states, rank)
    )
    picked = jnp.take(summed, distant_row_factor_index[:, 1], axis=0)
    far_out = jnp.einsum(
        "psr,plr->psl", picked, distant_row_factors, preferred_element_type=jnp.float32
    )
    all_out = jnp.concatenate([near_out, far_out], axis=0)
    all_rows = jnp.concatenate([near_rows, distant_row_factor_index[:, 0] - row_index * row_span])
    scatter = (all_rows[None, :] == jnp.arange(row_span, dtype=jnp.int32)[:, None]).astype(
        jnp.float32
    )
    partial_sum = jnp.dot(
        scatter, all_out.reshape(all_out.shape[0], states * leaf), precision=lax.Precision.HIGHEST
    ).reshape(row_span, states, leaf)
    partial_sum = partial_sum.transpose(1, 0, 2).reshape(states, row_span * leaf)
    return lax.psum_scatter(partial_sum, "col", scatter_dimension=0, tiled=True)


def solution(mesh):
    placed = (
        P("row", "col"),
        P("col"),
        P(("row", "col"), None, None),
        P(("row", "col"), None),
        P(("row", "col"), None, None),
        P(("row", "col"), None),
        P(("row", "col"), None, None),
        P(("row", "col"), None),
    )
    return jax.shard_map(
        per_device, mesh=mesh, in_specs=placed, out_specs=P("col", "row"), check_vma=False
    )
```

profile of v0, /device:TPU:0, one launch (start us, length us, event | category | flops | bytes accessed | tf_op | source)
XLA Modules:
  0.0 132.6 jit_solution(3973920628634587530)
XLA Ops:
  6.5 0.9 fusion.17
  7.5 0.8 compare_and_fusion
  8.2 2.6 %copy.16 = bf16[4,8192]{0,1:T(8,128)(2,1)} copy(bf16[4,8192]{1,0:T(4,128)(2,1)} %param.8) | data formatting | bytes 131072 | tf_op args[0]
  10.8 30.1 %gather_fusion = bf16[8192,4]{1,0:T(8,128)(2,1)} fusion(bf16[4,8192]{0,1:T(8,128)(2,1)} %copy.16, s32[8192]{0:T(1024)S(1)} %fusion.17), kind=kCustom, calls=%fused_computation | custom fusion | bytes 163840 | tf_op jit(solution)/shard_map/jit(_take)/gather | solution.py:38
  40.9 6.6 %bitcast_select_fusion = bf16[1,4,8192]{1,2,0:T(8,128)(2,1)} fusion(bf16[8192,4]{1,0:T(8,128)(2,1)} %gather_fusion, pred[8192]{0:T(1024)(128)(4,1)S(1)} %compare_and_fusion), kind=kLoop, calls=%fused_computation.4 | loop fusion | flops 32768 | bytes 139264 | tf_op jit(solution)/shard_map/jit(_take)/select_n | solution.py:38
  47.4 2.0 %copy.17 = bf16[1,4,8192]{2,1,0:T(4,128)(2,1)S(1)} copy(bf16[1,4,8192]{1,2,0:T(8,128)(2,1)} %bitcast_select_fusion) | data formatting | bytes 131072 | tf_op jit(solution)/shard_map/jit(_take)/select_n | solution.py:38
  49.4 15.6 %all_gather.7 = bf16[4,4,8192]{2,1,0:T(4,128)(2,1)S(1)} all-gather(bf16[1,4,8192]{2,1,0:T(4,128)(2,1)S(1)} %copy.17), channel_id=1, replica_groups=mesh['row'=8,'col'=4] {'col'}, dimensions={0}, use_global_device_ids=true | all-gather | bytes 327680 | tf_op jit(solution)/shard_map/all_gather | solution.py:41
  65.4 0.8 all_to_all.6
  66.2 4.1 %all-to-all-start = ((bf16[8,4,4864]{2,1,0:T(4,128)(2,1)}), bf16[8,4,4864]{2,1,0:T(4,128)(2,1)}, u32[]{:S(2)}, u32[]{:S(2)}) async-start(bf16[8,4,4864]{2,1,0:T(4,128)(2,1)} %all_to_all.6), calls=%async_computation | async-start | bytes 622592 | tf_op jit(solution)/shard_map/all_to_all | solution.py:50
  70.4 6.6 %fusion = bf16[1,4,8192]{1,2,0:T(8,128)(2,1)} fusion(bf16[8192,4]{1,0:T(8,128)(2,1)} %gather_fusion, pred[8192]{0:T(1024)(128)(4,1)S(1)} %compare_and_fusion), kind=kLoop, calls=%fused_computation.6 | loop fusion | flops 32768 | bytes 139264
  77.1 2.0 %copy.19 = bf16[1,4,8192]{2,1,0:T(4,128)(2,1)S(1)} copy(bf16[1,4,8192]{1,2,0:T(8,128)(2,1)} %fusion) | data formatting | bytes 131072
  79.0 10.2 %all-gather = bf16[8,4,8192]{2,1,0:T(4,128)(2,1)S(1)} all-gather(bf16[1,4,8192]{2,1,0:T(4,128)(2,1)S(1)} %copy.19), channel_id=1, replica_groups=mesh['row'=8,'col'=4] {'row'}, dimensions={0}, use_global_device_ids=true | all-gather | bytes 589824 | tf_op jit(solution)/shard_map/all_gather | solution.py:39
  89.2 1.2 reshape.75
  90.4 1.3 %copy.20 = bf16[32,32,256]{2,0,1:T(8,128)(2,1)S(1)} copy(bf16[32,32,256]{2,1,0:T(8,128)(2,1)} %reshape.75) | data formatting | bytes 1048576 | tf_op jit(solution)/shard_map/reshape | solution.py:40
  92.4 1.4 %fusion.3 = f32[30,32,32]{2,1,0:T(8,128)S(1)} fusion(bf16[30,256,32]{1,2,0:T(8,128)(2,1)} %param.14, bf16[30,32,256]{2,1,0:T(8,128)(2,1)S(1)} %gather_fusion.2, pred[30]{0:T(512)(128)(4,1)S(1)} %get-tuple-element.7), kind=kOutput, calls=%fused_computation.12 | convolution fusion | flops 15974400 | bytes 1105950 | tf_op jit(solution)/shard_map/spk,pkr->psr/dot_general | solution.py:64
  94.4 0.6 gather_fusion.3
  95.0 1.4 %fusion.12 = f32[30,32,256]{2,1,0:T(8,128)S(1)} fusion(bf16[30,256,32]{1,2,0:T(8,128)(2,1)} %param.12, bf16[30,32,32]{2,1,0:T(8,128)(2,1)S(1)} %gather_fusion.3, pred[30]{0:T(512)(128)(4,1)S(1)} %and_bitcast_fusion.1), kind=kOutput, calls=%fused_computation.21 | convolution fusion | flops 15759360 | bytes 1536030 | tf_op jit(solution)/shard_map/psr,plr->psl/dot_general | solution.py:82
  96.4 1.2 reshape.74
  97.5 0.8 copy.18
  98.3 1.5 %gather_fusion.1 = bf16[16,32,256]{2,1,0:T(8,128)(2,1)S(1)} fusion(bf16[32,19,256]{2,0,1:T(8,128)(2,1)} %copy.18, s32[1024]{0:T(1024)S(1)} %pad_clamp_fusion.2), kind=kCustom, calls=%fused_computation.1 | custom fusion | bytes 524352 | tf_op jit(solution)/shard_map/jit(_take)/gather | solution.py:57
  99.8 0.7 fusion.7
  100.8 1.5 %fusion.1 = f32[16,32,256]{2,0,1:T(8,128)S(1)} fusion(f32[32,256,46]{1,0,2:T(8,128)S(1)} %slice_bitcast_fusion, s32[46]{0:T(128)S(1)} %pad_add_fusion), kind=kOutput, calls=%fused_computation.7 | convolution fusion | flops 72352480 | bytes 2031800 | tf_op jit(solution)/shard_map/dot_general | solution.py:90
  102.3 1.1 copy.24
  103.4 22.4 %reduce-scatter.2.cloned.1.call-done = f32[8,4096]{1,0:T(8,128)} async-done(((f32[32,4096]{1,0:T(8,128)}), f32[8,4096]{1,0:T(8,128)}) %reduce-scatter.2.cloned.1.call-update) | async-done | bytes 131088 | tf_op jit(solution)/shard_map/reduce_scatter | solution.py:94
  (29 shorter events, 1.8 us)
Async XLA Ops:
  6.5 93.3 %copy-start = (bf16[16,256,256]{2,1,0:T(8,128)(2,1)S(1)}, bf16[16,256,256]{2,1,0:T(8,128)(2,1)}, u32[]{:S(2)}) copy-start(bf16[16,256,256]{2,1,0:T(8,128)(2,1)} %param.10) | copy-start | bytes 6291460
  66.2 30.2 %all-to-all-start = ((bf16[8,4,4864]{2,1,0:T(4,128)(2,1)}), bf16[8,4,4864]{2,1,0:T(4,128)(2,1)}, u32[]{:S(2)}, u32[]{:S(2)}) async-start(bf16[8,4,4864]{2,1,0:T(4,128)(2,1)} %all_to_all.6), calls=%async_computation | async-start | bytes 622592 | tf_op jit(solution)/shard_map/all_to_all | solution.py:50
  70.3 55.5 %reduce-scatter.2.cloned.1.call-start = ((), (), s32[]{:S(2)}) async-start(), calls=%async_computation.2 | async-start | bytes 655360 | tf_op jit(solution)/shard_map/reduce_scatter | solution.py:94
  70.3 6.6 %copy-start.1 = (s32[30,2]{0,1:T(2,128)S(1)}, s32[30,2]{0,1:T(2,128)}, u32[]{:S(2)}) copy-start(s32[30,2]{0,1:T(2,128)} %param.13) | copy-start | bytes 724
  70.3 6.6 %copy-start.2 = (s32[16,2]{0,1:T(2,128)S(1)}, s32[16,2]{0,1:T(2,128)}, u32[]{:S(2)}) copy-start(s32[16,2]{0,1:T(2,128)} %param.11) | copy-start | bytes 388
  77.0 14.7 %copy-start.3 = (s32[30,2]{0,1:T(2,128)S(1)}, s32[30,2]{0,1:T(2,128)}, u32[]{:S(2)}) copy-start(s32[30,2]{0,1:T(2,128)} %param.15) | copy-start | bytes 724
Sparse Core Ops, SparseCore 0:
  103.5 22.2 reduce-scatter.1
where the time goes:
time: 133 us
  local copies, waits for them, and re-layouts  46.4 us (35%)
  blocking collectives  25.8 us (19%)
  waiting for transfers between devices  22.4 us (17%)
  other arithmetic  15.1 us (11%)
  between operations  13.7 us (10%)
  matrix products  5.1 us (4%)
  starting transfers between devices  4.12 us (3%)
    gather x1, local copies, waits for them, and re-layouts, per_device(): mine = jnp.take(magnetic_potential_input, local_order, axis=1)  30.1 us
    reduce_scatter x1, waiting for transfers between devices, per_device(): return lax.psum_scatter(partial_sum, 'col', scatter_dimension=0, tiled=True)  22.4 us
    all_gather x1, blocking collectives, per_device(): every_block = lax.all_gather(mine, 'col', axis=0, tiled=False)  15.6 us
    all_gather x1, blocking collectives, per_device(): ordered = lax.all_gather(mine, 'row', axis=0, tiled=True)  10.2 us
    unnamed x1, other arithmetic  6.58 us
    select_n x1, other arithmetic, per_device(): mine = jnp.take(magnetic_potential_input, local_order, axis=1)  6.55 us
    unnamed x11, local copies, waits for them, and re-layouts  5.71 us
    all_to_all x1, starting transfers between devices, per_device(): lax.all_to_all(send, 'row', 0, 0, tiled=True).reshape(states, window, leaf)  4.08 us
  transfers between devices with their start and end apart: 2, of which 1 were waited for; matrix products, arithmetic and copies ran while one was open for 12% of the time, Pallas kernels for 0%

commit v1 on v0

--- a/solution.py
+++ b/solution.py
@@ -5,6 +5,19 @@
 
 BL = 2
 REACH = 3
+
+
+def gather_around(x, axis, dim):
+    ways = lax.axis_size(axis)
+    up = [(d, (d + 1) % ways) for d in range(ways)]
+    down = [(d, (d - 1) % ways) for d in range(ways)]
+    earlier, later = ([x], [x])
+    for _ in range(ways // 2):
+        earlier.append(lax.ppermute(earlier[-1], axis, up))
+    for _ in range((ways - 1) // 2):
+        later.append(lax.ppermute(later[-1], axis, down))
+    line = jnp.concatenate([*earlier[::-1], *later[1:]], axis=dim)
+    return jnp.roll(line, (lax.axis_index(axis) - ways // 2) * x.shape[dim], axis=dim)
 
 
 def per_device(
@@ -36,7 +49,7 @@
     block_entries = 4 * BL
     local_order = node_reordering - col_index * width
     mine = jnp.take(magnetic_potential_input, local_order, axis=1)
-    ordered = lax.all_gather(mine, "row", axis=0, tiled=True)
+    ordered = gather_around(mine, "row", 0)
     leaf_clusters = ordered.reshape(states, cluster_extent, leaf)
     every_block = lax.all_gather(mine, "col", axis=0, tiled=False)
     pieces = []

time: 133 us -> 189 us (1.42); the launches traced: 133 us -> 186 us
  local copies, waits for them, and re-layouts: 46.4 us -> 93.2 us
  blocking collectives: 25.8 us -> 14.8 us
  starting transfers between devices: 4.12 us -> 13 us
  waiting for transfers between devices: 22.4 us -> 30.9 us
    concatenate x0 -> x1, local copies, waits for them, and re-layouts: none -> 31 us  [gather_around(): jnp.roll(line, (lax.axis_index(axis) - ways // 2) * x.shape[dim], axis=dim)]
    ppermute x0 -> x7, local copies, waits for them, and re-layouts: none -> 13 us  [the longest x4 7.44 us: gather_around(): earlier.append(lax.ppermute(earlier[-1], axis, up))]
    all_gather x1 -> x0, blocking collectives: 10.2 us -> none  [per_device(): ordered = lax.all_gather(mine, 'row', axis=0, tiled=True)]
    ppermute x0 -> x7, starting transfers between devices: none -> 8.89 us  [the longest x3 8.03 us: gather_around(): later.append(lax.ppermute(later[-1], axis, down))]
    ppermute x0 -> x7, waiting for transfers between devices: none -> 7.86 us  [the longest x4 7.85 us: gather_around(): earlier.append(lax.ppermute(earlier[-1], axis, up))]
    select_n x1 -> x2, other arithmetic: 6.55 us -> 13.1 us  [per_device(): mine = jnp.take(magnetic_potential_input, local_order, axis=1)]
    unnamed x1 -> x0, other arithmetic: 6.58 us -> none
    dynamic_slice x0 -> x1, local copies, waits for them, and re-layouts: none -> 3.57 us  [gather_around(): jnp.roll(line, (lax.axis_index(axis) - ways // 2) * x.shape[dim], axis=dim)]
  transfers between devices with their start and end apart: 2 -> 9, of which waited for: 1 -> 3; matrix products, arithmetic and copies ran while one was open for 12% -> 34% of each run, Pallas kernels for 0% -> 0%
where the time goes in v1:
time: 189 us; the launch traced here: 186 us
  local copies, waits for them, and re-layouts  93.2 us (49%)
  waiting for transfers between devices  30.9 us (16%)
  other arithmetic  15.1 us (8%)
  blocking collectives  14.8 us (8%)
  between operations  13.7 us (7%)
  starting transfers between devices  13 us (7%)
  matrix products  5.1 us (3%)
    concatenate x1, local copies, waits for them, and re-layouts, gather_around(): jnp.roll(line, (lax.axis_index(axis) - ways // 2) * x.shape[dim], axis=dim)  31 us
    gather x1, local copies, waits for them, and re-layouts, per_device(): mine = jnp.take(magnetic_potential_input, local_order, axis=1)  29.8 us
    reduce_scatter x1, waiting for transfers between devices, per_device(): return lax.psum_scatter(partial_sum, 'col', scatter_dimension=0, tiled=True)  23.1 us
    all_gather x1, blocking collectives, per_device(): every_block = lax.all_gather(mine, 'col', axis=0, tiled=False)  14.8 us
    select_n x2, other arithmetic, per_device(): mine = jnp.take(magnetic_potential_input, local_order, axis=1)  13.1 us
    ppermute x3, starting transfers between devices, gather_around(): later.append(lax.ppermute(later[-1], axis, down))  8.03 us
    ppermute x4, waiting for transfers between devices, gather_around(): earlier.append(lax.ppermute(earlier[-1], axis, up))  7.85 us
    ppermute x4, local copies, waits for them, and re-layouts, gather_around(): earlier.append(lax.ppermute(earlier[-1], axis, up))  7.44 us
  transfers between devices with their start and end apart: 9, of which 3 were waited for; matrix products, arithmetic and copies ran while one was open for 34% of the time, Pallas kernels for 0%

profile of v1, /device:TPU:0, one launch (start us, length us, event | category | flops | bytes accessed | tf_op | source)
XLA Modules:
  0.0 185.8 jit_solution(1590735510283200097)
XLA Ops:
  8.2 2.6 %copy.20 = bf16[4,8192]{0,1:T(8,128)(2,1)} copy(bf16[4,8192]{1,0:T(4,128)(2,1)} %param.8) | data formatting | bytes 131072 | tf_op args[0]
  10.8 29.8 %gather_fusion = bf16[8192,4]{1,0:T(8,128)(2,1)} fusion(bf16[4,8192]{0,1:T(8,128)(2,1)} %copy.20, s32[8192]{0:T(1024)S(1)} %fusion.16), kind=kCustom, calls=%fused_computation | custom fusion | bytes 163840 | tf_op jit(solution)/shard_map/jit(_take)/gather | solution.py:51
  40.7 6.6 %bitcast_select_fusion.1 = bf16[4,8192]{0,1:T(8,128)(2,1)} fusion(bf16[8192,4]{1,0:T(8,128)(2,1)} %gather_fusion, pred[8192]{0:T(1024)(128)(4,1)S(1)} %compare_and_fusion), kind=kLoop, calls=%fused_computation.5 | loop fusion | flops 32768 | bytes 139264 | tf_op jit(solution)/shard_map/jit(_take)/select_n | solution.py:51
  47.3 2.0 %copy.23 = bf16[4,8192]{1,0:T(4,128)(2,1)S(1)} copy(bf16[4,8192]{0,1:T(8,128)(2,1)} %bitcast_select_fusion.1) | data formatting | bytes 131072 | tf_op jit(solution)/shard_map/jit(_take)/select_n | solution.py:51
  49.8 2.9 %collective-permute-start.4 = (bf16[4,8192]{1,0:T(4,128)(2,1)S(1)}, bf16[4,8192]{1,0:T(4,128)(2,1)S(1)}, u32[]{:S(2)}, u32[]{:S(2)}) collective-permute-start(bf16[4,8192]{1,0:T(4,128)(2,1)S(1)} %copy.23), channel_id=1, source_target_pairs={{0,28},{4,0},{8,4},{12,8},{16,12},{20,16},{24,20},{28,24},{1,29},{... | collective-permute-start | bytes 196616 | tf_op jit(solution)/shard_map/ppermute | solution.py:18
  52.7 6.6 %bitcast_select_fusion = bf16[1,4,8192]{1,2,0:T(8,128)(2,1)} fusion(bf16[8192,4]{1,0:T(8,128)(2,1)} %gather_fusion, pred[8192]{0:T(1024)(128)(4,1)S(1)} %compare_and_fusion), kind=kLoop, calls=%fused_computation.4 | loop fusion | flops 32768 | bytes 139264 | tf_op jit(solution)/shard_map/jit(_take)/select_n | solution.py:51
  59.3 2.0 %copy.21 = bf16[1,4,8192]{2,1,0:T(4,128)(2,1)S(1)} copy(bf16[1,4,8192]{1,2,0:T(8,128)(2,1)} %bitcast_select_fusion) | data formatting | bytes 131072 | tf_op jit(solution)/shard_map/jit(_take)/select_n | solution.py:51
  61.3 14.8 %all_gather.4 = bf16[4,4,8192]{2,1,0:T(4,128)(2,1)S(1)} all-gather(bf16[1,4,8192]{2,1,0:T(4,128)(2,1)S(1)} %copy.21), channel_id=1, replica_groups=mesh['row'=8,'col'=4] {'col'}, dimensions={0}, use_global_device_ids=true | all-gather | bytes 327680 | tf_op jit(solution)/shard_map/all_gather | solution.py:54
  77.2 4.1 %all-to-all-start = ((bf16[8,4,4864]{2,1,0:T(4,128)(2,1)}), bf16[8,4,4864]{2,1,0:T(4,128)(2,1)}, u32[]{:S(2)}, u32[]{:S(2)}) async-start(bf16[8,4,4864]{2,1,0:T(4,128)(2,1)} %all_to_all.6), calls=%async_computation | async-start | bytes 622592 | tf_op jit(solution)/shard_map/all_to_all | solution.py:63
  81.9 2.4 %collective-permute-start.5 = (bf16[4,8192]{1,0:T(4,128)(2,1)S(1)}, bf16[4,8192]{1,0:T(4,128)(2,1)S(1)}, u32[]{:S(2)}, u32[]{:S(2)}) collective-permute-start(bf16[4,8192]{1,0:T(4,128)(2,1)S(1)} %collective-permute-done.4), channel_id=1, source_target_pairs={{0,28},{4,0},{8,4},{12,8},{16,12},{20,16},{24,20},{28,24},{1,29},{... | collective-permute-start | bytes 196616 | tf_op jit(solution)/shard_map/ppermute | solution.py:18
  84.3 5.3 %collective-permute-done.1 = bf16[4,8192]{1,0:T(4,128)(2,1)S(1)} collective-permute-done((bf16[4,8192]{1,0:T(4,128)(2,1)S(1)}, bf16[4,8192]{1,0:T(4,128)(2,1)S(1)}, u32[]{:S(2)}, u32[]{:S(2)}) %collective-permute-start.1) | collective-permute-done | bytes 65568 | tf_op jit(solution)/shard_map/ppermute | solution.py:16
  89.6 2.7 %collective-permute-start.6 = (bf16[4,8192]{1,0:T(4,128)(2,1)S(1)}, bf16[4,8192]{1,0:T(4,128)(2,1)S(1)}, u32[]{:S(2)}, u32[]{:S(2)}) collective-permute-start(bf16[4,8192]{1,0:T(4,128)(2,1)S(1)} %collective-permute-done.5), channel_id=1, source_target_pairs={{0,28},{4,0},{8,4},{12,8},{16,12},{20,16},{24,20},{28,24},{1,29},{... | collective-permute-start | bytes 196616 | tf_op jit(solution)/shard_map/ppermute | solution.py:18
  92.3 2.6 %collective-permute-done.2 = bf16[4,8192]{1,0:T(4,128)(2,1)S(1)} collective-permute-done((bf16[4,8192]{1,0:T(4,128)(2,1)S(1)}, bf16[4,8192]{1,0:T(4,128)(2,1)S(1)}, u32[]{:S(2)}, u32[]{:S(2)}) %collective-permute-start.2) | collective-permute-done | bytes 65568 | tf_op jit(solution)/shard_map/ppermute | solution.py:16
  94.9 1.9 %copy.28 = bf16[4,8192]{0,1:T(8,128)(2,1)} copy(bf16[4,8192]{1,0:T(4,128)(2,1)S(1)} %collective-permute-done) | data formatting | bytes 131072 | tf_op jit(solution)/shard_map/ppermute | solution.py:16
  96.8 1.8 copy.29
  98.6 1.8 copy.27
  100.4 1.8 copy.30
  102.3 1.9 %copy.26 = bf16[4,8192]{0,1:T(8,128)(2,1)} copy(bf16[4,8192]{1,0:T(4,128)(2,1)S(1)} %collective-permute-done.2) | data formatting | bytes 131072 | tf_op jit(solution)/shard_map/ppermute | solution.py:16
  104.2 1.9 %copy.31 = bf16[4,8192]{0,1:T(8,128)(2,1)} copy(bf16[4,8192]{1,0:T(4,128)(2,1)S(1)} %collective-permute-done.6) | data formatting | bytes 131072 | tf_op jit(solution)/shard_map/ppermute | solution.py:18
  106.0 1.9 %copy.25 = bf16[4,8192]{0,1:T(8,128)(2,1)} copy(bf16[4,8192]{1,0:T(4,128)(2,1)S(1)} %collective-permute-done.3) | data formatting | bytes 131072 | tf_op jit(solution)/shard_map/ppermute | solution.py:16
  107.9 31.0 %concatenate.17 = bf16[64,8192]{0,1:T(8,128)(2,1)} concatenate(bf16[4,8192]{0,1:T(8,128)(2,1)} %copy.25, bf16[4,8192]{0,1:T(8,128)(2,1)} %copy.26, bf16[4,8192]{0,1:T(8,128)(2,1)} %copy.27, bf16[4,8192]{0,1:T(8,128)(2,1)} %copy.28, bf16[4,8192]{0,1:T(8,128)(2,1)} %bitcast_select_fusion.1, bf16[4,8192]{0,1:T(8,128)(2,1)} %copy.29, bf16[4,8192]{0,1:T(8,128)(2,1)} %copy.30, ...), dimensions={0} | concatenate | bytes 2097152 | tf_op jit(solution)/shard_map/jit(_roll_dynamic)/concatenate | solution.py:20
  138.9 3.6 %constant_dynamic-slice_fusion = bf16[32,8192]{0,1:T(8,128)(2,1)} fusion(bf16[64,8192]{0,1:T(8,128)(2,1)} %concatenate.17, s32[]{:T(128)S(6)} %select_n.76), kind=kLoop, calls=%fused_computation.54 | loop fusion | bytes 1048580 | tf_op jit(solution)/shard_map/jit(_roll_dynamic)/dynamic_slice | solution.py:20
  142.5 1.9 %copy.40 = bf16[32,32,256]{2,0,1:T(8,128)(2,1)S(1)} copy(bf16[32,32,256]{0,2,1:T(8,128)(2,1)} %bitcast.66) | data formatting | bytes 1048576 | tf_op jit(solution)/shard_map/reshape | solution.py:53
  155.9 23.1 %reduce-scatter.2.cloned.1.call-done = f32[8,4096]{1,0:T(8,128)} async-done(((f32[32,4096]{1,0:T(8,128)}), f32[8,4096]{1,0:T(8,128)}) %reduce-scatter.2.cloned.1.call-update) | async-done | bytes 131088 | tf_op jit(solution)/shard_map/reduce_scatter | solution.py:107
  (50 shorter events, 15.3 us)
Async XLA Ops:
  6.5 145.8 %copy-start = (bf16[16,256,256]{2,1,0:T(8,128)(2,1)S(1)}, bf16[16,256,256]{2,1,0:T(8,128)(2,1)}, u32[]{:S(2)}) copy-start(bf16[16,256,256]{2,1,0:T(8,128)(2,1)} %param.10) | copy-start | bytes 6291460
  49.2 32.3 %collective-permute-start = (bf16[4,8192]{1,0:T(4,128)(2,1)S(1)}, bf16[4,8192]{1,0:T(4,128)(2,1)S(1)}, u32[]{:S(2)}, u32[]{:S(2)}) collective-permute-start(bf16[4,8192]{1,0:T(4,128)(2,1)S(1)} %copy.23), channel_id=1, source_target_pairs={{0,4},{4,8},{8,12},{12,16},{16,20},{20,24},{24,28},{28,0},{1,5},{5... | collective-permute-start | bytes 196616 | tf_op jit(solution)/shard_map/ppermute | solution.py:16
  49.8 32.1 %collective-permute-start.4 = (bf16[4,8192]{1,0:T(4,128)(2,1)S(1)}, bf16[4,8192]{1,0:T(4,128)(2,1)S(1)}, u32[]{:S(2)}, u32[]{:S(2)}) collective-permute-start(bf16[4,8192]{1,0:T(4,128)(2,1)S(1)} %copy.23), channel_id=1, source_target_pairs={{0,28},{4,0},{8,4},{12,8},{16,12},{20,16},{24,20},{28,24},{1,29},{... | collective-permute-start | bytes 196616 | tf_op jit(solution)/shard_map/ppermute | solution.py:18
  59.3 22.1 %copy-start.1 = (s32[30,2]{0,1:T(2,128)S(1)}, s32[30,2]{0,1:T(2,128)}, u32[]{:S(2)}) copy-start(s32[30,2]{0,1:T(2,128)} %param.13) | copy-start | bytes 724
  59.3 22.2 %copy-start.2 = (s32[16,2]{0,1:T(2,128)S(1)}, s32[16,2]{0,1:T(2,128)}, u32[]{:S(2)}) copy-start(s32[16,2]{0,1:T(2,128)} %param.11) | copy-start | bytes 388
  59.3 22.2 %copy-start.3 = (s32[30,2]{0,1:T(2,128)S(1)}, s32[30,2]{0,1:T(2,128)}, u32[]{:S(2)}) copy-start(s32[30,2]{0,1:T(2,128)} %param.15) | copy-start | bytes 724
  77.2 71.6 %all-to-all-start = ((bf16[8,4,4864]{2,1,0:T(4,128)(2,1)}), bf16[8,4,4864]{2,1,0:T(4,128)(2,1)}, u32[]{:S(2)}, u32[]{:S(2)}) async-start(bf16[8,4,4864]{2,1,0:T(4,128)(2,1)} %all_to_all.6), calls=%async_computation | async-start | bytes 622592 | tf_op jit(solution)/shard_map/all_to_all | solution.py:63
  81.3 97.7 %reduce-scatter.2.cloned.1.call-start = ((), (), s32[]{:S(2)}) async-start(), calls=%async_computation.2 | async-start | bytes 655360 | tf_op jit(solution)/shard_map/reduce_scatter | solution.py:107
  81.5 8.0 %collective-permute-start.1 = (bf16[4,8192]{1,0:T(4,128)(2,1)S(1)}, bf16[4,8192]{1,0:T(4,128)(2,1)S(1)}, u32[]{:S(2)}, u32[]{:S(2)}) collective-permute-start(bf16[4,8192]{1,0:T(4,128)(2,1)S(1)} %collective-permute-done), channel_id=1, source_target_pairs={{0,4},{4,8},{8,12},{12,16},{16,20},{20,24},{24,28},{28,0},{1,5},{5... | collective-permute-start | bytes 196616 | tf_op jit(solution)/shard_map/ppermute | solution.py:16
  81.9 7.7 %collective-permute-start.5 = (bf16[4,8192]{1,0:T(4,128)(2,1)S(1)}, bf16[4,8192]{1,0:T(4,128)(2,1)S(1)}, u32[]{:S(2)}, u32[]{:S(2)}) collective-permute-start(bf16[4,8192]{1,0:T(4,128)(2,1)S(1)} %collective-permute-done.4), channel_id=1, source_target_pairs={{0,28},{4,0},{8,4},{12,8},{16,12},{20,16},{24,20},{28,24},{1,29},{... | collective-permute-start | bytes 196616 | tf_op jit(solution)/shard_map/ppermute | solution.py:18
  89.6 5.3 %collective-permute-start.2 = (bf16[4,8192]{1,0:T(4,128)(2,1)S(1)}, bf16[4,8192]{1,0:T(4,128)(2,1)S(1)}, u32[]{:S(2)}, u32[]{:S(2)}) collective-permute-start(bf16[4,8192]{1,0:T(4,128)(2,1)S(1)} %collective-permute-done.1), channel_id=1, source_target_pairs={{0,4},{4,8},{8,12},{12,16},{16,20},{20,24},{24,28},{28,0},{1,5},{5... | collective-permute-start | bytes 196616 | tf_op jit(solution)/shard_map/ppermute | solution.py:16
  89.6 14.6 %collective-permute-start.6 = (bf16[4,8192]{1,0:T(4,128)(2,1)S(1)}, bf16[4,8192]{1,0:T(4,128)(2,1)S(1)}, u32[]{:S(2)}, u32[]{:S(2)}) collective-permute-start(bf16[4,8192]{1,0:T(4,128)(2,1)S(1)} %collective-permute-done.5), channel_id=1, source_target_pairs={{0,28},{4,0},{8,4},{12,8},{16,12},{20,16},{24,20},{28,24},{1,29},{... | collective-permute-start | bytes 196616 | tf_op jit(solution)/shard_map/ppermute | solution.py:18
  94.9 11.2 %collective-permute-start.3 = (bf16[4,8192]{1,0:T(4,128)(2,1)S(1)}, bf16[4,8192]{1,0:T(4,128)(2,1)S(1)}, u32[]{:S(2)}, u32[]{:S(2)}) collective-permute-start(bf16[4,8192]{1,0:T(4,128)(2,1)S(1)} %collective-permute-done.2), channel_id=1, source_target_pairs={{0,4},{4,8},{8,12},{12,16},{16,20},{20,24},{24,28},{28,0},{1,5},{5... | collective-permute-start | bytes 196616 | tf_op jit(solution)/shard_map/ppermute | solution.py:16
Sparse Core Ops, SparseCore 0:
  156.0 22.8 reduce-scatter.1
